TPU v7x, 256 devices: a whole 4x4x8 slice. The times are simulated.
256 devices in a mesh: wide: 16 (over z, core), narrow: 16 (over y, x).
Axes of the slice: x: 4, y: 4, z: 8, core: 2. Of those that a mesh axis runs over, the one named last changes fastest.
Arguments:
- screens: bfloat16 [4, 4096, 4096], P(None, 'wide'), may hold values from -3 to 3
- offsets: int32 [2, 128, 4], replicated, may hold values from 0 to 2752, as said below
- valid: int32 [2, 80, 80], P(None, 'narrow'), may hold values from 0 to 1, as said below
- recon: bfloat16 [25600, 5120], P('narrow', 'wide'), may hold values from -0.0390625 to 0.0390625
Outputs:
- slopes: float32 [2, 64, 2, 80, 80], P(None, 'wide', None, 'narrow')
- commands: float32 [64, 5120], P('narrow', 'wide')
Inputs may be any that keep to these rules, and one draw needn't show every extreme that they name: For each coordinate and each layer, the offsets of all items lie within 64 of the smallest, and the largest is exactly 64 above the smallest. In the 5 subaperture rows of one index of narrow, each sensor has at most 300 valid subapertures; in every draw one index of narrow holds exactly 300 for each sensor.
All inputs are finite; a program needn't handle non-finite values.
Results may differ from a plain program's by a relative error of at most 0.0043.
Values may be sent and summed in bfloat16 or wider, within the bound.
No kernel may reach another device: no remote copies, remote signals or barrier semaphores. Data moves between devices by JAX's collectives and lax.ppermute only.
A program may use at most 128 MiB of HBM per device.

v0:
```python
import math
import jax
import jax.numpy as jnp
from jax import lax
from jax.sharding import PartitionSpec as P

L = 4
NSUB = 80
SAMP = 16
NPIX = 32
NSENS = 2
SPREAD = 64
FR_DEV = 4
PUP = 1280


def broadcast(block, axis, source):
    block = jnp.where(lax.axis_index(axis) == source, block, jnp.zeros_like(block))
    return lax.psum(block, axis)


def dft_table(samp, npix):
    sample_ids = jnp.arange(samp * samp, dtype=jnp.int32)
    pixel_ids = jnp.arange(npix * npix, dtype=jnp.int32)
    sample_row = sample_ids // samp
    sample_col = sample_ids % samp
    pixel_row = pixel_ids // npix - npix // 2
    pixel_col = pixel_ids % npix - npix // 2
    phase_turns = jnp.mod(
        sample_row[:, None] * pixel_row[None, :] + sample_col[:, None] * pixel_col[None, :], npix
    )
    angles = phase_turns.astype(jnp.float32) * jnp.float32(-2.0 * math.pi / npix)
    cosine = jnp.cos(angles).astype(jnp.bfloat16)
    sine_part = jnp.sin(angles).astype(jnp.bfloat16)
    top_rows = jnp.concatenate([cosine, sine_part], axis=1)
    bottom_rows = jnp.concatenate([-sine_part, cosine], axis=1)
    return jnp.concatenate([top_rows, bottom_rows], axis=0)


def subaperture_fields(pupil_phase, samp):
    sub_rows = pupil_phase.shape[0] // samp
    sub_cols = pupil_phase.shape[1] // samp
    samples = (
        pupil_phase.reshape(sub_rows, samp, sub_cols, samp)
        .transpose(0, 2, 1, 3)
        .reshape(sub_rows * sub_cols, samp * samp)
    )
    return jnp.concatenate([jnp.cos(samples), jnp.sin(samples)], axis=1).astype(jnp.bfloat16)


def centroids(fields, transform, npix):
    spectrum = jnp.dot(fields, transform, preferred_element_type=jnp.float32)
    pixel_count = npix * npix
    real_part = spectrum[:, :pixel_count]
    imag_part = spectrum[:, pixel_count:]
    intensity = real_part * real_part + imag_part * imag_part
    pixel_ids = jnp.arange(pixel_count, dtype=jnp.int32)
    along_x = (pixel_ids % npix - npix // 2).astype(jnp.float32)
    along_y = (pixel_ids // npix - npix // 2).astype(jnp.float32)
    flux_total = jnp.sum(intensity, axis=1)
    centre_x = jnp.sum(intensity * along_x[None, :], axis=1) / flux_total
    centre_y = jnp.sum(intensity * along_y[None, :], axis=1) / flux_total
    return jnp.stack([centre_x, centre_y], axis=1)


def body(screens, offsets, valid, recon):
    narrow_count = lax.axis_size("narrow")
    wide_index = lax.axis_index("wide")
    narrow_index = lax.axis_index("narrow")
    band_rows = screens.shape[1]
    sub_rows = valid.shape[1]
    pixel_rows = sub_rows * SAMP
    slab_rows = pixel_rows + SPREAD
    union_cols = PUP + SPREAD
    local_items = FR_DEV * NSENS
    own_offsets = lax.dynamic_slice_in_dim(offsets, wide_index * local_items, local_items, 1)
    lowest = jnp.min(offsets, axis=1)
    pad = jnp.zeros((slab_rows, union_cols), screens.dtype)
    slabs = []
    for which_layer in range(L):
        band = lax.dynamic_slice_in_dim(screens[which_layer], lowest[1, which_layer], union_cols, 1)
        padded = jnp.concatenate([pad, band, pad], axis=0)
        group_start = lowest[0, which_layer] + pixel_rows * narrow_index
        row_at = jnp.clip(
            group_start - wide_index * band_rows + slab_rows, 0, band_rows + slab_rows
        )
        slabs.append(lax.dynamic_slice_in_dim(padded, row_at, slab_rows, 0))
    slabs = lax.psum(jnp.stack(slabs), "wide")
    rel = own_offsets - lowest[:, None, :]
    phases = []
    for item in range(local_items):
        acc = jnp.zeros((pixel_rows, PUP), jnp.float32)
        for which_layer in range(L):
            window = lax.dynamic_slice(
                slabs[which_layer],
                (rel[0, item, which_layer], rel[1, item, which_layer]),
                (pixel_rows, PUP),
            )
            acc = acc + window.astype(jnp.float32)
        phases.append(acc)
    pupil_phase = jnp.stack(phases)
    transform = dft_table(SAMP, NPIX)
    frame_phase = pupil_phase.reshape(FR_DEV, NSENS, pixel_rows, PUP)
    valid_flags = valid.reshape(-1)

    def frame_fields(frame_block):
        return jnp.concatenate(
            [subaperture_fields(frame_block[sensor_index], SAMP) for sensor_index in range(NSENS)],
            axis=0,
        )

    def one_frame(frame_block):
        return centroids(frame_fields(frame_block), transform, NPIX) * valid_flags[:, None].astype(
            jnp.float32
        )

    measured = lax.map(one_frame, frame_phase)
    measured = measured.reshape(FR_DEV, NSENS, sub_rows, NSUB, 2)
    slopes = measured.transpose(4, 0, 1, 2, 3)
    slope_vector = (
        measured.transpose(0, 2, 1, 3, 4)
        .reshape(FR_DEV, sub_rows * NSENS * NSUB * 2)
        .astype(jnp.bfloat16)
    )
    partial_commands = jnp.dot(
        lax.all_gather(slope_vector, "wide", axis=0, tiled=True),
        recon,
        preferred_element_type=jnp.float32,
    )
    partial_commands = partial_commands.reshape(narrow_count, -1, partial_commands.shape[1])
    commands = jnp.sum(lax.all_to_all(partial_commands, "narrow", 0, 0), axis=0)
    return (slopes, commands)


def solution(mesh):
    return jax.shard_map(
        body,
        mesh=mesh,
        in_specs=(P(None, "wide", None), P(), P(None, "narrow", None), P("narrow", "wide")),
        out_specs=(P(None, "wide", None, "narrow", None), P("narrow", "wide")),
        check_vma=False,
    )
```

profile of v0, /device:TPU:1, one launch (start us, length us, event | category | flops | bytes accessed | tf_op | source)
XLA Modules:
  0.0 316.4 jit_solution(13882446086356264635)
XLA Ops:
  13.8 5.6 %fusion.50 = (bf16[1,256,4096]{2,1,0:T(8,128)(2,1)S(1)}, bf16[1,256,4096]{2,1,0:T(8,128)(2,1)}, bf16[1,256,4096]{2,1,0:T(8,128)(2,1)}, bf16[1,256,4096]{2,1,0:T(8,128)(2,1)}) fusion(bf16[4,256,4096]{2,1,0:T(8,128)(2,1)} %param.6), kind=kLoop, calls=%fused_computation.106 | loop fusion | bytes 16777216 | tf_op jit(solution)/shard_map/slice | solution.py:81
  24.4 2.3 dynamic-slice_bitcast_fusion
  28.8 3.2 %fusion.35 = (bf16[1,144,1344]{2,1,0:T(8,128)(2,1)S(1)}, bf16[1,144,1344]{2,1,0:T(8,128)(2,1)S(1)}, bf16[1,144,1344]{2,1,0:T(8,128)(2,1)S(1)}, bf16[1,144,1344]{2,1,0:T(8,128)(2,1)S(1)}) fusion(s32[]{:T(128)S(6)} %min.13, bf16[144,1344]{1,0:T(8,128)(2,1)S(1)} %broadcast_in_dim.6, bf16[256,1344]{1,0:T(8,128)(2,1)S(1)} %get-tuple-element.220, s32[]{:T(128)S(6)} %min.15, ...), kind=kLoop, calls=%fused_computation.80 | loop fusion | flops 4644864 | bytes 4687888 | tf_op jit(solution)/shard_map/stack | solution.py:88
  155.5 4.3 %fusion.48 = bf16[256,1024]{1,0:T(8,128)(2,1)S(1)} fusion(s32[1024]{0:T(1024)S(1)} %get-tuple-element.214, s32[256]{0:T(256)S(1)} %get-tuple-element.215, s32[1024]{0:T(1024)S(1)} %get-tuple-element.213, s32[256]{0:T(256)S(1)} %get-tuple-element.216), kind=kLoop, calls=%fused_computation.104 | loop fusion | flops 5242880 | bytes 534528 | tf_op jit(solution)/shard_map/neg | solution.py:36
  159.9 4.8 %sine_convert_fusion.2 = (bf16[256,1024]{1,0:T(8,128)(2,1)S(1)}, bf16[256,1024]{1,0:T(8,128)(2,1)S(1)}) fusion(s32[1024]{0:T(1024)S(1)} %get-tuple-element.214, s32[256]{0:T(256)S(1)} %get-tuple-element.215, s32[1024]{0:T(1024)S(1)} %get-tuple-element.213, s32[256]{0:T(256)S(1)} %get-tuple-element.216), kind=kLoop, calls=%fused_computation.55 | loop fusion | flops 4718592 | bytes 1058816 | tf_op jit(solution)/shard_map/convert_element_type | solution.py:34
  173.1 98.5 %while.13 = (s32[]{:T(128)}, f32[4,800,2]{1,2,0:T(2,128)S(1)}, f32[4,2,80,1280]{3,2,1,0:T(8,128)}, bf16[512,2048]{1,0:T(8,128)(2,1)}, f32[800,1]{0,1:T(1,128)S(1)}, /*index=5*/s32[]{:T(128)}, s32[]{:T(128)}, s32[]{}, f32[]{:T(128)}) while((s32[]{:T(128)}, f32[4,800,2]{1,2,0:T(2,128)S(1)}, f32[4,2,80,1280]{3,2,1,0:T(8,128)}, ...), condition=%wide.region_6.7_spmd, body=%wide.region_2.6_spmd.sunk | while | flops 1687980416 | bytes 22656888 | solution.py:117
  173.1 5.2 %cosine_convert_fusion.4 = (bf16[1,1,80,1280]{3,2,1,0:T(8,128)(2,1)}, bf16[1,1,80,1280]{3,2,1,0:T(8,128)(2,1)}, bf16[1,1,80,1280]{3,2,1,0:T(8,128)(2,1)S(1)}, bf16[1,1,80,1280]{3,2,1,0:T(8,128)(2,1)S(1)}) fusion(f32[4,2,80,1280]{3,2,1,0:T(8,128)} %get-tuple-element.294, s32[]{:T(128)} %get-tuple-element.283, s32[]{:T(128)S(6)} %add.637), kind=kLoop, calls=%fused_computation.16.clone.1 | loop fusion | flops 409600 | bytes 1638408 | tf_op jit(solution)/shard_map/convert.15
  181.6 2.2 cos.49
  185.8 2.2 sin.47
  192.7 3.8 %fusion.70 = f32[800,2048]{1,0:T(8,128)S(1)} fusion(bf16[512,2048]{1,0:T(8,128)(2,1)} %get-tuple-element.295, bf16[400,256]{0,1:T(8,128)(2,1)} %sin.48, bf16[400,256]{0,1:T(8,128)(2,1)} %cos.48, bf16[400,256]{0,1:T(8,128)(2,1)S(1)} %sin.50, bf16[400,256]{0,1:T(8,128)(2,1)} %cos.50), kind=kOutput, calls=%fused_computation.5.clone.1 | convolution fusion | flops 1680998400 | bytes 9469952 | tf_op jit(solution)/shard_map/while/body/eval_jaxpr/dot_general | solution.py:52
  197.7 5.2 %cosine_convert_fusion.4 = (bf16[1,1,80,1280]{3,2,1,0:T(8,128)(2,1)}, bf16[1,1,80,1280]{3,2,1,0:T(8,128)(2,1)}, bf16[1,1,80,1280]{3,2,1,0:T(8,128)(2,1)S(1)}, bf16[1,1,80,1280]{3,2,1,0:T(8,128)(2,1)S(1)}) fusion(f32[4,2,80,1280]{3,2,1,0:T(8,128)} %get-tuple-element.294, s32[]{:T(128)} %get-tuple-element.283, s32[]{:T(128)S(6)} %add.637), kind=kLoop, calls=%fused_computation.16.clone.1 | loop fusion | flops 409600 | bytes 1638408 | tf_op jit(solution)/shard_map/convert.15
  206.2 2.2 cos.49
  210.5 2.2 sin.47
  217.3 3.9 %fusion.70 = f32[800,2048]{1,0:T(8,128)S(1)} fusion(bf16[512,2048]{1,0:T(8,128)(2,1)} %get-tuple-element.295, bf16[400,256]{0,1:T(8,128)(2,1)} %sin.48, bf16[400,256]{0,1:T(8,128)(2,1)} %cos.48, bf16[400,256]{0,1:T(8,128)(2,1)S(1)} %sin.50, bf16[400,256]{0,1:T(8,128)(2,1)} %cos.50), kind=kOutput, calls=%fused_computation.5.clone.1 | convolution fusion | flops 1680998400 | bytes 9469952 | tf_op jit(solution)/shard_map/while/body/eval_jaxpr/dot_general | solution.py:52
  222.4 5.2 %cosine_convert_fusion.4 = (bf16[1,1,80,1280]{3,2,1,0:T(8,128)(2,1)}, bf16[1,1,80,1280]{3,2,1,0:T(8,128)(2,1)}, bf16[1,1,80,1280]{3,2,1,0:T(8,128)(2,1)S(1)}, bf16[1,1,80,1280]{3,2,1,0:T(8,128)(2,1)S(1)}) fusion(f32[4,2,80,1280]{3,2,1,0:T(8,128)} %get-tuple-element.294, s32[]{:T(128)} %get-tuple-element.283, s32[]{:T(128)S(6)} %add.637), kind=kLoop, calls=%fused_computation.16.clone.1 | loop fusion | flops 409600 | bytes 1638408 | tf_op jit(solution)/shard_map/convert.15
  230.8 2.2 cos.49
  235.1 2.2 sin.47
  241.9 3.9 %fusion.70 = f32[800,2048]{1,0:T(8,128)S(1)} fusion(bf16[512,2048]{1,0:T(8,128)(2,1)} %get-tuple-element.295, bf16[400,256]{0,1:T(8,128)(2,1)} %sin.48, bf16[400,256]{0,1:T(8,128)(2,1)} %cos.48, bf16[400,256]{0,1:T(8,128)(2,1)S(1)} %sin.50, bf16[400,256]{0,1:T(8,128)(2,1)} %cos.50), kind=kOutput, calls=%fused_computation.5.clone.1 | convolution fusion | flops 1680998400 | bytes 9469952 | tf_op jit(solution)/shard_map/while/body/eval_jaxpr/dot_general | solution.py:52
  247.0 5.2 %cosine_convert_fusion.4 = (bf16[1,1,80,1280]{3,2,1,0:T(8,128)(2,1)}, bf16[1,1,80,1280]{3,2,1,0:T(8,128)(2,1)}, bf16[1,1,80,1280]{3,2,1,0:T(8,128)(2,1)S(1)}, bf16[1,1,80,1280]{3,2,1,0:T(8,128)(2,1)S(1)}) fusion(f32[4,2,80,1280]{3,2,1,0:T(8,128)} %get-tuple-element.294, s32[]{:T(128)} %get-tuple-element.283, s32[]{:T(128)S(6)} %add.637), kind=kLoop, calls=%fused_computation.16.clone.1 | loop fusion | flops 409600 | bytes 1638408 | tf_op jit(solution)/shard_map/convert.15
  255.5 2.2 cos.49
  266.6 3.8 %fusion.70 = f32[800,2048]{1,0:T(8,128)S(1)} fusion(bf16[512,2048]{1,0:T(8,128)(2,1)} %get-tuple-element.295, bf16[400,256]{0,1:T(8,128)(2,1)} %sin.48, bf16[400,256]{0,1:T(8,128)(2,1)} %cos.48, bf16[400,256]{0,1:T(8,128)(2,1)S(1)} %sin.50, bf16[400,256]{0,1:T(8,128)(2,1)} %cos.50), kind=kOutput, calls=%fused_computation.5.clone.1 | convolution fusion | flops 1680998400 | bytes 9469952 | tf_op jit(solution)/shard_map/while/body/eval_jaxpr/dot_general | solution.py:52
  272.3 21.9 %all-gather = bf16[16,4,1600]{2,1,0:T(4,128)(2,1)S(1)} all-gather(bf16[1,4,1600]{2,1,0:T(4,128)(2,1)S(1)} %copy.28), channel_id=1, replica_groups=mesh['wide'=16,'narrow'=16] {'wide'}, dimensions={0}, use_global_device_ids=true | all-gather | bytes 217600 | tf_op jit(solution)/shard_map/all_gather | solution.py:126
  295.5 6.8 %all-to-all-start = ((f32[16,4,320]{2,1,0:T(4,128)}), f32[16,4,320]{2,1,0:T(4,128)S(1)}, u32[]{:S(2)}, u32[]{:S(2)}) async-start(f32[16,4,320]{2,1,0:T(4,128)} %reshape.294), calls=%async_computation | async-start | bytes 196608 | tf_op jit(solution)/shard_map/all_to_all | solution.py:131
  302.9 6.0 %all-to-all-done = f32[16,4,320]{2,1,0:T(4,128)S(1)} async-done(((f32[16,4,320]{2,1,0:T(4,128)}), f32[16,4,320]{2,1,0:T(4,128)S(1)}, u32[]{:S(2)}, u32[]{:S(2)}) %all-to-all-start) | async-done | bytes 81952 | tf_op jit(solution)/shard_map/all_to_all | solution.py:131
  (115 shorter events, 66.0 us)
Async XLA Ops:
  7.2 287.2 %copy-start = (bf16[1600,320]{0,1:T(8,128)(2,1)S(1)}, bf16[1600,320]{0,1:T(8,128)(2,1)}, u32[]{:S(2)}) copy-start(bf16[1600,320]{0,1:T(8,128)(2,1)} %param.9) | copy-start | bytes 3072004
  7.2 159.0 %all-reduce.2.cloned.1.call-start = ((), (), s32[]{:S(2)}) async-start(), calls=%async_computation.1 | async-start | bytes 3244032 | tf_op jit(solution)/shard_map/psum | solution.py:88
  32.0 1.5 copy-start.2
  32.0 83.7 %copy-start.3 = (s32[2,5,80]{2,0,1:T(2,128)S(1)}, s32[2,5,80]{2,0,1:T(2,128)}, u32[]{:S(2)}) copy-start(s32[2,5,80]{2,0,1:T(2,128)} %param.8) | copy-start | bytes 9604
  171.4 1.7 copy-start.1
  295.5 13.5 %all-to-all-start = ((f32[16,4,320]{2,1,0:T(4,128)}), f32[16,4,320]{2,1,0:T(4,128)S(1)}, u32[]{:S(2)}, u32[]{:S(2)}) async-start(f32[16,4,320]{2,1,0:T(4,128)} %reshape.294), calls=%async_computation | async-start | bytes 196608 | tf_op jit(solution)/shard_map/all_to_all | solution.py:131
Sparse Core Ops, SparseCore 0:
  33.6 116.6 all-reduce.1
where the time goes:
time: 320 us; the launch traced here: 316 us
  between operations  143 us (45%)
  local copies, waits for them, and re-layouts  76 us (24%)
  other arithmetic  46 us (14%)
  blocking collectives  21.9 us (7%)
  matrix products  15.8 us (5%)
  starting transfers between devices  6.82 us (2%)
  waiting for transfers between devices  6.04 us (2%)
    cos x24, local copies, waits for them, and re-layouts, subaperture_fields(): jnp.cos(samples)  30.1 us
    sin x24, local copies, waits for them, and re-layouts, subaperture_fields(): jnp.sin(samples)  27.1 us
    all_gather x1, blocking collectives, body(): lax.all_gather(slope_vector, 'wide', axis=0, tiled=True)  21.9 us
    another operation x8, other arithmetic  20.9 us
    dot_general x4, matrix products, centroids(): spectrum = jnp.dot(fields, transform, preferred_element_type=jnp.float32)  15.4 us
    all_to_all x1, starting transfers between devices, body(): commands = jnp.sum(lax.all_to_all(partial_commands, 'narrow', 0, 0), axis=0)  6.79 us
  transfers between devices with their start and end apart: 2, of which 1 were waited for; matrix products, arithmetic and copies ran while one was open for 5% of the time, Pallas kernels for 0%

commit v1 on v0

--- a/solution.py
+++ b/solution.py
@@ -64,6 +64,12 @@
 
 
 def body(screens, offsets, valid, recon):
+
+    def fix_desk(my_tile):
+        mixed_arr = lax.all_to_all(jnp.stack([my_tile] * lax.axis_size("wide")), "wide", 0, 0)
+        b_now = jnp.concatenate(mixed_arr, 0)
+        return b_now
+
     narrow_count = lax.axis_size("narrow")
     wide_index = lax.axis_index("wide")
     narrow_index = lax.axis_index("narrow")
@@ -122,11 +128,7 @@
         .reshape(FR_DEV, sub_rows * NSENS * NSUB * 2)
         .astype(jnp.bfloat16)
     )
-    partial_commands = jnp.dot(
-        lax.all_gather(slope_vector, "wide", axis=0, tiled=True),
-        recon,
-        preferred_element_type=jnp.float32,
-    )
+    partial_commands = jnp.dot(fix_desk(slope_vector), recon, preferred_element_type=jnp.float32)
     partial_commands = partial_commands.reshape(narrow_count, -1, partial_commands.shape[1])
     commands = jnp.sum(lax.all_to_all(partial_commands, "narrow", 0, 0), axis=0)
     return (slopes, commands)

time: 320 us -> 319 us (level)
    all_gather x1 -> x0, blocking collectives: 21.9 us -> none  [body(): lax.all_gather(slope_vector, 'wide', axis=0, tiled=True)]
    all_to_all x0 -> x1, blocking collectives: none -> 20.5 us  [fix_desk(): lax.all_to_all(jnp.stack([my_tile] * lax.axis_size('wide')), 'wide', 0, 0)]
where the time goes in v1:
time: 319 us; the launch traced here: 315 us
  between operations  143 us (45%)
  local copies, waits for them, and re-layouts  76 us (24%)
  other arithmetic  46 us (14%)
  blocking collectives  20.5 us (6%)
  matrix products  15.8 us (5%)
  starting transfers between devices  6.78 us (2%)
  waiting for transfers between devices  6.52 us (2%)
    cos x24, local copies, waits for them, and re-layouts, subaperture_fields(): jnp.cos(samples)  30.1 us
    sin x24, local copies, waits for them, and re-layouts, subaperture_fields(): jnp.sin(samples)  27.1 us
    another operation x8, other arithmetic  20.9 us
    all_to_all x1, blocking collectives, fix_desk(): lax.all_to_all(jnp.stack([my_tile] * lax.axis_size('wide')), 'wide', 0, 0)  20.5 us
    dot_general x4, matrix products, centroids(): spectrum = jnp.dot(fields, transform, preferred_element_type=jnp.float32)  15.4 us
    all_to_all x1, starting transfers between devices, body(): commands = jnp.sum(lax.all_to_all(partial_commands, 'narrow', 0, 0), axis=0)  6.74 us
    all_to_all x1, waiting for transfers between devices, body(): commands = jnp.sum(lax.all_to_all(partial_commands, 'narrow', 0, 0), axis=0)  6.51 us
  transfers between devices with their start and end apart: 2, of which 1 were waited for; matrix products, arithmetic and copies ran while one was open for 5% of the time, Pallas kernels for 0%

profile of v1, /device:TPU:1, one launch (start us, length us, event | category | flops | bytes accessed | tf_op | source)
XLA Modules:
  0.0 315.4 jit_solution(17006792417511825724)
XLA Ops:
  13.8 5.6 %fusion.53 = (bf16[1,256,4096]{2,1,0:T(8,128)(2,1)S(1)}, bf16[1,256,4096]{2,1,0:T(8,128)(2,1)}, bf16[1,256,4096]{2,1,0:T(8,128)(2,1)}, bf16[1,256,4096]{2,1,0:T(8,128)(2,1)}) fusion(bf16[4,256,4096]{2,1,0:T(8,128)(2,1)} %param.6), kind=kLoop, calls=%fused_computation.109 | loop fusion | bytes 16777216 | tf_op jit(solution)/shard_map/slice | solution.py:87
  24.4 2.3 dynamic-slice_bitcast_fusion
  28.8 3.2 %fusion.37 = (bf16[1,144,1344]{2,1,0:T(8,128)(2,1)S(1)}, bf16[1,144,1344]{2,1,0:T(8,128)(2,1)S(1)}, bf16[1,144,1344]{2,1,0:T(8,128)(2,1)S(1)}, bf16[1,144,1344]{2,1,0:T(8,128)(2,1)S(1)}) fusion(s32[]{:T(128)S(6)} %min.13, bf16[144,1344]{1,0:T(8,128)(2,1)S(1)} %broadcast_in_dim.6, bf16[256,1344]{1,0:T(8,128)(2,1)S(1)} %get-tuple-element.218, s32[]{:T(128)S(6)} %min.15, ...), kind=kLoop, calls=%fused_computation.82 | loop fusion | flops 4644864 | bytes 4687888 | tf_op jit(solution)/shard_map/stack | solution.py:94
  155.5 4.3 %fusion.51 = bf16[256,1024]{1,0:T(8,128)(2,1)S(1)} fusion(s32[1024]{0:T(1024)S(1)} %get-tuple-element.212, s32[256]{0:T(256)S(1)} %get-tuple-element.213, s32[1024]{0:T(1024)S(1)} %get-tuple-element.211, s32[256]{0:T(256)S(1)} %get-tuple-element.214), kind=kLoop, calls=%fused_computation.107 | loop fusion | flops 5242880 | bytes 534528 | tf_op jit(solution)/shard_map/neg | solution.py:36
  159.9 4.8 %sine_convert_fusion.2 = (bf16[256,1024]{1,0:T(8,128)(2,1)S(1)}, bf16[256,1024]{1,0:T(8,128)(2,1)S(1)}) fusion(s32[1024]{0:T(1024)S(1)} %get-tuple-element.212, s32[256]{0:T(256)S(1)} %get-tuple-element.213, s32[1024]{0:T(1024)S(1)} %get-tuple-element.211, s32[256]{0:T(256)S(1)} %get-tuple-element.214), kind=kLoop, calls=%fused_computation.57 | loop fusion | flops 4718592 | bytes 1058816 | tf_op jit(solution)/shard_map/convert_element_type | solution.py:34
  173.1 98.5 %while.13 = (s32[]{:T(128)}, f32[4,800,2]{1,2,0:T(2,128)S(1)}, f32[4,2,80,1280]{3,2,1,0:T(8,128)}, bf16[512,2048]{1,0:T(8,128)(2,1)}, f32[800,1]{0,1:T(1,128)S(1)}, /*index=5*/s32[]{:T(128)}, s32[]{:T(128)}, s32[]{}, f32[]{:T(128)}) while((s32[]{:T(128)}, f32[4,800,2]{1,2,0:T(2,128)S(1)}, f32[4,2,80,1280]{3,2,1,0:T(8,128)}, ...), condition=%wide.region_6.7_spmd, body=%wide.region_2.6_spmd.sunk | while | flops 1687980416 | bytes 22656888 | solution.py:123
  173.1 5.2 %cosine_convert_fusion.4 = (bf16[1,1,80,1280]{3,2,1,0:T(8,128)(2,1)}, bf16[1,1,80,1280]{3,2,1,0:T(8,128)(2,1)}, bf16[1,1,80,1280]{3,2,1,0:T(8,128)(2,1)S(1)}, bf16[1,1,80,1280]{3,2,1,0:T(8,128)(2,1)S(1)}) fusion(f32[4,2,80,1280]{3,2,1,0:T(8,128)} %get-tuple-element.292, s32[]{:T(128)} %get-tuple-element.281, s32[]{:T(128)S(6)} %add.637), kind=kLoop, calls=%fused_computation.16.clone.1 | loop fusion | flops 409600 | bytes 1638408 | tf_op jit(solution)/shard_map/convert.15
  181.6 2.2 cos.49
  185.8 2.2 sin.47
  192.7 3.8 %fusion.70 = f32[800,2048]{1,0:T(8,128)S(1)} fusion(bf16[512,2048]{1,0:T(8,128)(2,1)} %get-tuple-element.293, bf16[400,256]{0,1:T(8,128)(2,1)} %sin.48, bf16[400,256]{0,1:T(8,128)(2,1)} %cos.48, bf16[400,256]{0,1:T(8,128)(2,1)S(1)} %sin.50, bf16[400,256]{0,1:T(8,128)(2,1)} %cos.50), kind=kOutput, calls=%fused_computation.5.clone.1 | convolution fusion | flops 1680998400 | bytes 9469952 | tf_op jit(solution)/shard_map/while/body/eval_jaxpr/dot_general | solution.py:52
  197.7 5.2 %cosine_convert_fusion.4 = (bf16[1,1,80,1280]{3,2,1,0:T(8,128)(2,1)}, bf16[1,1,80,1280]{3,2,1,0:T(8,128)(2,1)}, bf16[1,1,80,1280]{3,2,1,0:T(8,128)(2,1)S(1)}, bf16[1,1,80,1280]{3,2,1,0:T(8,128)(2,1)S(1)}) fusion(f32[4,2,80,1280]{3,2,1,0:T(8,128)} %get-tuple-element.292, s32[]{:T(128)} %get-tuple-element.281, s32[]{:T(128)S(6)} %add.637), kind=kLoop, calls=%fused_computation.16.clone.1 | loop fusion | flops 409600 | bytes 1638408 | tf_op jit(solution)/shard_map/convert.15
  206.2 2.2 cos.49
  210.5 2.2 sin.47
  217.3 3.9 %fusion.70 = f32[800,2048]{1,0:T(8,128)S(1)} fusion(bf16[512,2048]{1,0:T(8,128)(2,1)} %get-tuple-element.293, bf16[400,256]{0,1:T(8,128)(2,1)} %sin.48, bf16[400,256]{0,1:T(8,128)(2,1)} %cos.48, bf16[400,256]{0,1:T(8,128)(2,1)S(1)} %sin.50, bf16[400,256]{0,1:T(8,128)(2,1)} %cos.50), kind=kOutput, calls=%fused_computation.5.clone.1 | convolution fusion | flops 1680998400 | bytes 9469952 | tf_op jit(solution)/shard_map/while/body/eval_jaxpr/dot_general | solution.py:52
  222.4 5.2 %cosine_convert_fusion.4 = (bf16[1,1,80,1280]{3,2,1,0:T(8,128)(2,1)}, bf16[1,1,80,1280]{3,2,1,0:T(8,128)(2,1)}, bf16[1,1,80,1280]{3,2,1,0:T(8,128)(2,1)S(1)}, bf16[1,1,80,1280]{3,2,1,0:T(8,128)(2,1)S(1)}) fusion(f32[4,2,80,1280]{3,2,1,0:T(8,128)} %get-tuple-element.292, s32[]{:T(128)} %get-tuple-element.281, s32[]{:T(128)S(6)} %add.637), kind=kLoop, calls=%fused_computation.16.clone.1 | loop fusion | flops 409600 | bytes 1638408 | tf_op jit(solution)/shard_map/convert.15
  230.8 2.2 cos.49
  235.1 2.2 sin.47
  241.9 3.9 %fusion.70 = f32[800,2048]{1,0:T(8,128)S(1)} fusion(bf16[512,2048]{1,0:T(8,128)(2,1)} %get-tuple-element.293, bf16[400,256]{0,1:T(8,128)(2,1)} %sin.48, bf16[400,256]{0,1:T(8,128)(2,1)} %cos.48, bf16[400,256]{0,1:T(8,128)(2,1)S(1)} %sin.50, bf16[400,256]{0,1:T(8,128)(2,1)} %cos.50), kind=kOutput, calls=%fused_computation.5.clone.1 | convolution fusion | flops 1680998400 | bytes 9469952 | tf_op jit(solution)/shard_map/while/body/eval_jaxpr/dot_general | solution.py:52
  247.0 5.2 %cosine_convert_fusion.4 = (bf16[1,1,80,1280]{3,2,1,0:T(8,128)(2,1)}, bf16[1,1,80,1280]{3,2,1,0:T(8,128)(2,1)}, bf16[1,1,80,1280]{3,2,1,0:T(8,128)(2,1)S(1)}, bf16[1,1,80,1280]{3,2,1,0:T(8,128)(2,1)S(1)}) fusion(f32[4,2,80,1280]{3,2,1,0:T(8,128)} %get-tuple-element.292, s32[]{:T(128)} %get-tuple-element.281, s32[]{:T(128)S(6)} %add.637), kind=kLoop, calls=%fused_computation.16.clone.1 | loop fusion | flops 409600 | bytes 1638408 | tf_op jit(solution)/shard_map/convert.15
  255.5 2.2 cos.49
  266.6 3.8 %fusion.70 = f32[800,2048]{1,0:T(8,128)S(1)} fusion(bf16[512,2048]{1,0:T(8,128)(2,1)} %get-tuple-element.293, bf16[400,256]{0,1:T(8,128)(2,1)} %sin.48, bf16[400,256]{0,1:T(8,128)(2,1)} %cos.48, bf16[400,256]{0,1:T(8,128)(2,1)S(1)} %sin.50, bf16[400,256]{0,1:T(8,128)(2,1)} %cos.50), kind=kOutput, calls=%fused_computation.5.clone.1 | convolution fusion | flops 1680998400 | bytes 9469952 | tf_op jit(solution)/shard_map/while/body/eval_jaxpr/dot_general | solution.py:52
  272.4 20.5 %all_to_all.10 = bf16[16,4,1600]{2,1,0:T(4,128)(2,1)S(1)} all-to-all(bf16[16,4,1600]{2,1,0:T(4,128)(2,1)S(1)} %stack.29), channel_id=1, replica_groups=mesh['wide'=16,'narrow'=16] {'wide'}, dimensions={0} | all-to-all | bytes 409600 | tf_op jit(solution)/shard_map/all_to_all | solution.py:69
  294.0 6.7 %all-to-all-start.1 = ((f32[16,4,320]{2,1,0:T(4,128)}), f32[16,4,320]{2,1,0:T(4,128)S(1)}, u32[]{:S(2)}, u32[]{:S(2)}) async-start(f32[16,4,320]{2,1,0:T(4,128)} %copy.23), calls=%async_computation.1 | async-start | bytes 196608 | tf_op jit(solution)/shard_map/all_to_all | solution.py:133
  301.4 6.5 %all-to-all-done.1 = f32[16,4,320]{2,1,0:T(4,128)S(1)} async-done(((f32[16,4,320]{2,1,0:T(4,128)}), f32[16,4,320]{2,1,0:T(4,128)S(1)}, u32[]{:S(2)}, u32[]{:S(2)}) %all-to-all-start.1) | async-done | bytes 81952 | tf_op jit(solution)/shard_map/all_to_all | solution.py:133
  (115 shorter events, 66.0 us)
Async XLA Ops:
  7.2 285.8 %copy-start = (bf16[1600,320]{0,1:T(8,128)(2,1)S(1)}, bf16[1600,320]{0,1:T(8,128)(2,1)}, u32[]{:S(2)}) copy-start(bf16[1600,320]{0,1:T(8,128)(2,1)} %param.9) | copy-start | bytes 3072004
  7.2 159.0 %all-reduce.2.cloned.1.call-start = ((), (), s32[]{:S(2)}) async-start(), calls=%async_computation.2 | async-start | bytes 3244032 | tf_op jit(solution)/shard_map/psum | solution.py:94
  32.0 1.5 copy-start.2
  32.0 83.7 %copy-start.3 = (s32[2,5,80]{2,0,1:T(2,128)S(1)}, s32[2,5,80]{2,0,1:T(2,128)}, u32[]{:S(2)}) copy-start(s32[2,5,80]{2,0,1:T(2,128)} %param.8) | copy-start | bytes 9604
  171.4 1.7 copy-start.1
  294.0 13.9 %all-to-all-start.1 = ((f32[16,4,320]{2,1,0:T(4,128)}), f32[16,4,320]{2,1,0:T(4,128)S(1)}, u32[]{:S(2)}, u32[]{:S(2)}) async-start(f32[16,4,320]{2,1,0:T(4,128)} %copy.23), calls=%async_computation.1 | async-start | bytes 196608 | tf_op jit(solution)/shard_map/all_to_all | solution.py:133
Sparse Core Ops, SparseCore 0:
  33.6 116.6 all-reduce.1
